TPU v7x, 32 devices: a whole 2x2x4 slice. The times are simulated.
32 devices in a mesh: slab: 4 (over y, x), rad: 8 (over z, core).
Axes of the slice: x: 2, y: 2, z: 4, core: 2. Of those that a mesh axis runs over, the one named last changes fastest.
Arguments:
- q_state: float32 [3, 524288], P(None, ('slab', 'rad')), may hold values from -6.71 to 6.71, as said below
- increments: float32 [3, 524288], P(None, ('slab', 'rad')), may hold values from -6 to 6
- velocity_grad: float32 [5, 12288], P(None, 'slab'), may hold values from -40 to 40
- element: int32 [524288], P(('slab', 'rad')), may hold values from 0 to 3071
- migration: int32 [524288], P(('slab', 'rad')), may hold values from -1 to 1, as said below
- volume: float32 [12288], P(('slab', 'rad')), may hold values from 14.222222 to 128
- div_map: float32 [192, 192], replicated, may hold values from -0.4375 to 0.4375
- stiffness: float32 [256, 4, 192, 192], P(('slab', 'rad')), may hold values from -0.06 to 1.06
- pattern: int32 [256, 4], P(('slab', 'rad')), may hold values from 0 to 191, as said below
- preconditioner: float32 [256, 192, 192], P(('slab', 'rad')), may hold values from -0.03 to 1.03
Outputs:
- q_out: float32 [3, 524288], P(None, ('slab', 'rad'))
- arrivals: float32 [2, 3, 32768], P(None, None, ('slab', 'rad'))
- element_stress: float32 [4, 12288], P(None, ('slab', 'rad'))
- velocity: float32 [256, 192], P(('slab', 'rad'))
Inputs may be any that keep to these rules, and one draw needn't show every extreme that they name: `q_state`: every dumbbell's stretch r^2 + z^2 + t^2 is below 45. Of the dumbbells of one device at most 1024 have migration 1 and at most 1024 have migration -1; some device has exactly 1024 with 1 and some device exactly 1024 with -1. pattern[b, 0] = 64 + b % 64; pattern[b, 1] lies in 0 .. 63, pattern[b, 2] in 64 .. 127, pattern[b, 3] in 128 .. 191.
All inputs are finite; a program needn't handle non-finite values.
Results may differ from a plain program's by a relative error of at most 0.0003.
Values sent between devices are 32-bit elements; how exact they have to be, the bound alone decides.
No kernel may reach another device: no remote copies, remote signals or barrier semaphores. Data moves between devices by JAX's collectives and lax.ppermute only.
A program may use at most 64 MiB of HBM per device.

v0:
```python
import math
import jax
import jax.numpy as jnp
from jax import lax
from jax.sharding import PartitionSpec as P

BLOCK = 192
ITERS = 6
extensibility = 50.0
time_step = 0.01
noise_scale = 0.1
damping = 0.6
highest = lax.Precision.HIGHEST


def passed_along(array, axis, by):
    size = lax.axis_size(axis)
    pairs = [(i, i + by) for i in range(size) if 0 <= i + by < size]
    return lax.ppermute(array, axis, pairs)


def extended(cells, sides, width):
    for axis, dim in sides:
        count = lax.axis_size(axis)
        ends = count - 1
        head = lax.slice_in_dim(cells, 0, width, axis=dim)
        tail = lax.slice_in_dim(cells, cells.shape[dim] - width, cells.shape[dim], axis=dim)
        cells = jnp.concatenate(
            [
                lax.ppermute(tail, axis, [(i, (i + 1) % count) for i in range(ends)]),
                cells,
                lax.ppermute(head, axis, [((i + 1) % count, i) for i in range(ends)]),
            ],
            axis=dim,
        )
    return cells


def update_dumbbells(q_here, inc_here, grads):
    radial = q_here[0]
    axial = q_here[1]
    azimuth = q_here[2]
    stretch = radial * radial + axial * axial + azimuth * azimuth
    spring = 1.0 / (1.0 - stretch / extensibility)
    drift = jnp.stack(
        [
            grads[0] * radial + grads[1] * axial,
            grads[2] * radial + grads[3] * axial,
            grads[4] * azimuth,
        ]
    )
    q_next = q_here + time_step * (drift - 0.5 * spring * q_here) + noise_scale * inc_here
    terms = jnp.stack(
        [
            spring * radial * radial - 1.0,
            spring * axial * axial - 1.0,
            spring * radial * axial,
            spring * azimuth * azimuth - 1.0,
        ]
    )
    return (q_next, terms)


def block_size(count):
    return math.gcd(count, 2048)


def split_onehots(index, count):
    upper_part = index // 128
    lower_part = index % 128
    hot_upper = (upper_part[None, :] == jnp.arange(count // 128, dtype=jnp.int32)[:, None]).astype(
        jnp.float32
    )
    hot_lower = (lower_part[None, :] == jnp.arange(128, dtype=jnp.int32)[:, None]).astype(
        jnp.float32
    )
    return (hot_upper, hot_lower)


def lookup_columns(table, index):
    rows, count = table.shape
    groups = count // 128
    arranged = table.reshape(rows, groups, 128).transpose(0, 2, 1).reshape(rows * 128, groups)
    size = block_size(index.shape[0])

    def one_block(indices):
        hot_upper, hot_lower = split_onehots(indices, count)
        picked = jnp.dot(arranged, hot_upper, precision=highest).reshape(rows, 128, size)
        return jnp.sum(picked * hot_lower[None], 1)

    result = lax.map(one_block, index.reshape(-1, size))
    return result.transpose(1, 0, 2).reshape(rows, -1)


def spread_block(values, indices, count):
    rows, size = values.shape
    hot_upper, hot_lower = split_onehots(indices, count)
    spread = (values[:, None, :] * hot_lower[None]).reshape(rows * 128, size)
    return lax.dot_general(spread, hot_upper, (((1,), (1,)), ((), ())), precision=highest)


def unarrange(total, rows, count):
    return total.reshape(rows, 128, count // 128).transpose(0, 2, 1).reshape(rows, count)


def accumulate_columns(values, index, count):
    rows = values.shape[0]
    size = block_size(index.shape[0])

    def accumulate_step(total, items):
        block_values, block_index = items
        return (total + spread_block(block_values, block_index, count), None)

    start = jnp.zeros((rows * 128, count // 128), jnp.float32)
    blocks = (values.reshape(rows, -1, size).transpose(1, 0, 2), index.reshape(-1, size))
    total, unused = lax.scan(accumulate_step, start, blocks)
    return unarrange(total, rows, count)


def pack_both(payload, migration, capacity):
    rows = payload.shape[0]
    padded_cap = -(-capacity // 128) * 128
    size = block_size(migration.shape[0])
    positions = jnp.arange(size, dtype=jnp.int32)
    earlier = (positions[:, None] < positions[None, :]).astype(jnp.bfloat16)

    def pack_step(carry, items):
        offsets, totals = carry
        block_values, block_moves = items
        chosen = jnp.stack([block_moves == 1, block_moves == -1])
        ranks = jnp.dot(
            chosen.astype(jnp.bfloat16), earlier, preferred_element_type=jnp.float32
        ).astype(jnp.int32)
        slots = jnp.where(chosen, offsets[:, None] + ranks, 0)
        filled = []
        for direction in range(2):
            masked = jnp.where(chosen[direction][None], block_values, 0.0)
            filled.append(spread_block(masked, slots[direction], padded_cap))
        offsets = offsets + jnp.sum(chosen.astype(jnp.int32), 1)
        return ((offsets, totals + jnp.stack(filled)), None)

    start = (jnp.zeros((2,), jnp.int32), jnp.zeros((2, rows * 128, padded_cap // 128), jnp.float32))
    blocks = (payload.reshape(rows, -1, size).transpose(1, 0, 2), migration.reshape(-1, size))
    (offsets, totals), unused = lax.scan(pack_step, start, blocks)
    upward = unarrange(totals[0], rows, padded_cap)
    downward = unarrange(totals[1], rows, padded_cap)
    return (upward, downward)


def body(
    q_state,
    increments,
    velocity_grad,
    element,
    migration,
    volume,
    div_map,
    stiffness,
    pattern,
    preconditioner,
):
    capacity = migration.shape[0] // 16
    slab_elems = velocity_grad.shape[1]
    grads = lookup_columns(velocity_grad, element)
    q_next, terms = update_dumbbells(q_state, increments, grads)
    payload = jnp.concatenate([q_next, terms, element.astype(jnp.float32)[None]], 0)
    upward, downward = pack_both(payload, migration, capacity)
    from_lower = passed_along(upward, "slab", 1)
    from_upper = passed_along(downward, "slab", -1)
    staying = jnp.where(migration == 0, terms, 0.0)
    all_terms = jnp.concatenate([staying, from_lower[3:7], from_upper[3:7]], 1)
    all_index = jnp.concatenate(
        [element, from_lower[7].astype(jnp.int32), from_upper[7].astype(jnp.int32)], 0
    )
    partial_value = accumulate_columns(all_terms, all_index, slab_elems)
    sums = lax.psum_scatter(partial_value, "rad", scatter_dimension=1, tiled=True)
    element_stress = sums / volume
    arrivals = jnp.stack([from_lower[0:3], from_upper[0:3]])
    own_blocks = stiffness.shape[0]
    groups = (
        element_stress.reshape(4, own_blocks, BLOCK // 4)
        .transpose(1, 0, 2)
        .reshape(own_blocks, BLOCK)
    )
    force = jnp.dot(groups, div_map, precision=highest)

    def precondition(vector):
        return jnp.einsum("bij,bj->bi", preconditioner, vector, precision=highest)

    window_rows = 3 * own_blocks * lax.axis_size("rad")
    selector = (
        pattern.reshape(-1)[:, None] == jnp.arange(window_rows, dtype=jnp.int32)[None, :]
    ).astype(jnp.float32)
    velocity = damping * precondition(force)
    for sweep_index in range(1, ITERS):
        gathered = lax.all_gather(velocity, "rad", axis=0, tiled=True)
        window = extended(gathered, (("slab", 0),), gathered.shape[0])
        neighbours = jnp.dot(selector, window, precision=highest).reshape(own_blocks, -1, BLOCK)
        image = jnp.einsum("bnij,bnj->bi", stiffness, neighbours, precision=highest)
        velocity = velocity + damping * precondition(force - image)
    return (q_next, arrivals, element_stress, velocity)


def solution(mesh):
    placed = (
        P(None, ("slab", "rad")),
        P(None, ("slab", "rad")),
        P(None, "slab"),
        P(("slab", "rad")),
        P(("slab", "rad")),
        P(("slab", "rad")),
        P(),
        P(("slab", "rad"), None, None, None),
        P(("slab", "rad"), None),
        P(("slab", "rad"), None, None),
    )
    return jax.shard_map(
        body,
        mesh=mesh,
        in_specs=placed,
        out_specs=(
            P(None, ("slab", "rad")),
            P(None, None, ("slab", "rad")),
            P(None, ("slab", "rad")),
            P(("slab", "rad"), None),
        ),
        check_vma=False,
    )
```

profile of v0, /device:TPU:4, one launch (start us, length us, event | category | flops | bytes accessed | tf_op | source)
XLA Modules:
  0.0 413.1 jit_solution(11150976871779817177)
XLA Ops:
  11.6 26.4 %while.41 = (s32[]{:T(128)}, f32[8,5,2048]{2,1,0:T(8,128)S(1)}, s32[8,2048]{1,0:T(8,128)S(1)}, f32[640,24]{0,1:T(8,128)S(1)}, s32[]{:T(128)}) while((s32[]{:T(128)}, f32[8,5,2048]{2,1,0:T(8,128)S(1)}, s32[8,2048]{1,0:T(8,128)S(1)}, f32[640,24]{0,1:T(8,128)S(1)}, s32[]{:T(128)}) %tuple.140), condition=%wide.region_2.3_spmd, body=%wide.region_0.2_spmd.sunk | while | flops 380719104 | bytes 12882001 | solution.py:91
  39.7 92.5 %while.42 = (s32[]{:T(128)}, s32[2]{0:T(128)S(1)}, f32[2,1024,8]{1,2,0:T(8,128)S(1)}, s32[8,2048]{1,0:T(8,128)S(1)}, f32[8,8,2048]{2,1,0:T(8,128)S(1)}, /*index=5*/s32[]{:T(128)}, s32[]{:T(128)}) while((s32[]{:T(128)}, s32[2]{0:T(128)S(1)}, f32[2,1024,8]{1,2,0:T(8,128)S(1)}, s32[8,2048]{1,0:T(8,128)S(1)}, ...), condition=%wide.region_5.6_spmd.clone, body=%wide.region_3.5_spmd.clone.sunk | while | flops 433287168 | bytes 38502552 | solution.py:144
  142.7 62.6 %while.43 = (s32[]{:T(128)}, f32[512,24]{0,1:T(8,128)S(1)}, f32[9,4,2048]{2,0,1:T(8,128)S(1)}, s32[9,2048]{1,0:T(8,128)S(1)}, s32[]{:T(128)}, /*index=5*/s32[]{:T(128)}) while((s32[]{:T(128)}, f32[512,24]{0,1:T(8,128)S(1)}, f32[9,4,2048]{2,0,1:T(8,128)S(1)}, s32[9,2048]{1,0:T(8,128)S(1)}, s32[]{:T(128)}, ...), condition=%wide.region_7.8_spmd.clone, body=%wide.region_6.7_spmd.clone.sunk | while | flops 303677440 | bytes 10805343 | solution.py:116
  145.6 4.2 %convolution_add_fusion.2 = f32[512,24]{0,1:T(8,128)S(1)} fusion(f32[512,2048]{1,0:T(8,128)} %bitcast.207, s32[2048]{0:T(1024)S(1)} %bitcast.214, f32[512,24]{0,1:T(8,128)S(1)} %get-tuple-element.504, pred[]{:T(512)S(6)} %compare.47), kind=kOutput, calls=%fused_computation.14.clone.1 | convolution fusion | flops 302063616 | bytes 4300801 | tf_op jit(solution)/shard_map/while/body/eval_jaxpr/dot_general | solution.py:99
  152.6 4.2 %convolution_add_fusion.2 = f32[512,24]{0,1:T(8,128)S(1)} fusion(f32[512,2048]{1,0:T(8,128)} %bitcast.207, s32[2048]{0:T(1024)S(1)} %bitcast.214, f32[512,24]{0,1:T(8,128)S(1)} %get-tuple-element.504, pred[]{:T(512)S(6)} %compare.47), kind=kOutput, calls=%fused_computation.14.clone.1 | convolution fusion | flops 302063616 | bytes 4300801 | tf_op jit(solution)/shard_map/while/body/eval_jaxpr/dot_general | solution.py:99
  159.5 4.2 %convolution_add_fusion.2 = f32[512,24]{0,1:T(8,128)S(1)} fusion(f32[512,2048]{1,0:T(8,128)} %bitcast.207, s32[2048]{0:T(1024)S(1)} %bitcast.214, f32[512,24]{0,1:T(8,128)S(1)} %get-tuple-element.504, pred[]{:T(512)S(6)} %compare.47), kind=kOutput, calls=%fused_computation.14.clone.1 | convolution fusion | flops 302063616 | bytes 4300801 | tf_op jit(solution)/shard_map/while/body/eval_jaxpr/dot_general | solution.py:99
  166.4 4.2 %convolution_add_fusion.2 = f32[512,24]{0,1:T(8,128)S(1)} fusion(f32[512,2048]{1,0:T(8,128)} %bitcast.207, s32[2048]{0:T(1024)S(1)} %bitcast.214, f32[512,24]{0,1:T(8,128)S(1)} %get-tuple-element.504, pred[]{:T(512)S(6)} %compare.47), kind=kOutput, calls=%fused_computation.14.clone.1 | convolution fusion | flops 302063616 | bytes 4300801 | tf_op jit(solution)/shard_map/while/body/eval_jaxpr/dot_general | solution.py:99
  173.4 4.2 %convolution_add_fusion.2 = f32[512,24]{0,1:T(8,128)S(1)} fusion(f32[512,2048]{1,0:T(8,128)} %bitcast.207, s32[2048]{0:T(1024)S(1)} %bitcast.214, f32[512,24]{0,1:T(8,128)S(1)} %get-tuple-element.504, pred[]{:T(512)S(6)} %compare.47), kind=kOutput, calls=%fused_computation.14.clone.1 | convolution fusion | flops 302063616 | bytes 4300801 | tf_op jit(solution)/shard_map/while/body/eval_jaxpr/dot_general | solution.py:99
  180.3 4.2 %convolution_add_fusion.2 = f32[512,24]{0,1:T(8,128)S(1)} fusion(f32[512,2048]{1,0:T(8,128)} %bitcast.207, s32[2048]{0:T(1024)S(1)} %bitcast.214, f32[512,24]{0,1:T(8,128)S(1)} %get-tuple-element.504, pred[]{:T(512)S(6)} %compare.47), kind=kOutput, calls=%fused_computation.14.clone.1 | convolution fusion | flops 302063616 | bytes 4300801 | tf_op jit(solution)/shard_map/while/body/eval_jaxpr/dot_general | solution.py:99
  187.3 4.2 %convolution_add_fusion.2 = f32[512,24]{0,1:T(8,128)S(1)} fusion(f32[512,2048]{1,0:T(8,128)} %bitcast.207, s32[2048]{0:T(1024)S(1)} %bitcast.214, f32[512,24]{0,1:T(8,128)S(1)} %get-tuple-element.504, pred[]{:T(512)S(6)} %compare.47), kind=kOutput, calls=%fused_computation.14.clone.1 | convolution fusion | flops 302063616 | bytes 4300801 | tf_op jit(solution)/shard_map/while/body/eval_jaxpr/dot_general | solution.py:99
  194.2 4.2 %convolution_add_fusion.2 = f32[512,24]{0,1:T(8,128)S(1)} fusion(f32[512,2048]{1,0:T(8,128)} %bitcast.207, s32[2048]{0:T(1024)S(1)} %bitcast.214, f32[512,24]{0,1:T(8,128)S(1)} %get-tuple-element.504, pred[]{:T(512)S(6)} %compare.47), kind=kOutput, calls=%fused_computation.14.clone.1 | convolution fusion | flops 302063616 | bytes 4300801 | tf_op jit(solution)/shard_map/while/body/eval_jaxpr/dot_general | solution.py:99
  201.1 4.2 %convolution_add_fusion.2 = f32[512,24]{0,1:T(8,128)S(1)} fusion(f32[512,2048]{1,0:T(8,128)} %bitcast.207, s32[2048]{0:T(1024)S(1)} %bitcast.214, f32[512,24]{0,1:T(8,128)S(1)} %get-tuple-element.504, pred[]{:T(512)S(6)} %compare.47), kind=kOutput, calls=%fused_computation.14.clone.1 | convolution fusion | flops 302063616 | bytes 4300801 | tf_op jit(solution)/shard_map/while/body/eval_jaxpr/dot_general | solution.py:99
  207.1 34.3 %reduce-scatter.4.cloned.1.call-done = f32[384,4]{1,0:T(8,128)} async-done(((f32[3072,4]{1,0:T(8,128)}), f32[384,4]{1,0:T(8,128)}) %reduce-scatter.4.cloned.1.call-update) | async-done | bytes 6160
  244.2 14.0 %all_gather.15 = f32[64,192]{1,0:T(8,128)S(1)} all-gather(f32[8,192]{1,0:T(8,128)S(1)} %bitcast_multiply_fusion.5), channel_id=1, replica_groups=mesh['slab'=4,'rad'=8] {'rad'}, dimensions={0}, use_global_device_ids=true | all-gather | bytes 55296 | tf_op jit(solution)/shard_map/all_gather | solution.py:196
  264.4 4.5 %collective-permute-done.2 = f32[64,192]{1,0:T(8,128)S(1)} collective-permute-done((f32[64,192]{1,0:T(8,128)S(1)}, f32[64,192]{1,0:T(8,128)S(1)}, u32[]{:S(2)}, u32[]{:S(2)}) %collective-permute-start.2) | collective-permute-done | bytes 49184 | tf_op jit(solution)/shard_map/ppermute | solution.py:30
  269.1 7.2 %fusion.95 = f32[8,1,192,1]{2,1,3,0:T(1,128)S(1)} fusion(f32[8,4,192,1]{2,3,1,0:T(1,128)S(1)} %reshape.325, f32[8,4,192,192]{3,2,1,0:T(8,128)} %param.23), kind=kOutput, calls=%fused_computation.172 | convolution fusion | flops 14155776 | bytes 4749312 | tf_op jit(solution)/shard_map/bnij,bnj->bi/dot_general | solution.py:199
  277.7 14.0 %all_gather.16 = f32[64,192]{1,0:T(8,128)S(1)} all-gather(f32[8,192]{1,0:T(8,128)S(1)} %fusion.71), channel_id=1, replica_groups=mesh['slab'=4,'rad'=8] {'rad'}, dimensions={0}, use_global_device_ids=true | all-gather | bytes 55296 | tf_op jit(solution)/shard_map/all_gather | solution.py:196
  301.0 7.2 %fusion.96 = f32[8,1,192,1]{2,1,3,0:T(1,128)S(1)} fusion(f32[8,4,192,1]{2,3,1,0:T(1,128)S(1)} %reshape.327, f32[8,4,192,192]{3,2,1,0:T(8,128)} %param.23), kind=kOutput, calls=%fused_computation.173 | convolution fusion | flops 14155776 | bytes 4749312 | tf_op jit(solution)/shard_map/bnij,bnj->bi/dot_general | solution.py:199
  309.6 14.2 %all_gather.17 = f32[64,192]{1,0:T(8,128)S(1)} all-gather(f32[8,192]{1,0:T(8,128)S(1)} %fusion.69), channel_id=1, replica_groups=mesh['slab'=4,'rad'=8] {'rad'}, dimensions={0}, use_global_device_ids=true | all-gather | bytes 55296 | tf_op jit(solution)/shard_map/all_gather | solution.py:196
  333.1 7.2 %fusion.97 = f32[8,1,192,1]{2,1,3,0:T(1,128)S(1)} fusion(f32[8,4,192,1]{2,3,1,0:T(1,128)S(1)} %reshape.329, f32[8,4,192,192]{3,2,1,0:T(8,128)} %param.23), kind=kOutput, calls=%fused_computation.174 | convolution fusion | flops 14155776 | bytes 4749312 | tf_op jit(solution)/shard_map/bnij,bnj->bi/dot_general | solution.py:199
  341.7 14.0 %all_gather.18 = f32[64,192]{1,0:T(8,128)S(1)} all-gather(f32[8,192]{1,0:T(8,128)S(1)} %fusion.67), channel_id=1, replica_groups=mesh['slab'=4,'rad'=8] {'rad'}, dimensions={0}, use_global_device_ids=true | all-gather | bytes 55296 | tf_op jit(solution)/shard_map/all_gather | solution.py:196
  365.0 7.2 %fusion.98 = f32[8,1,192,1]{2,1,3,0:T(1,128)S(1)} fusion(f32[8,4,192,1]{2,3,1,0:T(1,128)S(1)} %reshape.331, f32[8,4,192,192]{3,2,1,0:T(8,128)} %param.23), kind=kOutput, calls=%fused_computation.175 | convolution fusion | flops 14155776 | bytes 4749312 | tf_op jit(solution)/shard_map/bnij,bnj->bi/dot_general | solution.py:199
  373.5 14.0 %all_gather.19 = f32[64,192]{1,0:T(8,128)S(1)} all-gather(f32[8,192]{1,0:T(8,128)S(1)} %fusion.65), channel_id=1, replica_groups=mesh['slab'=4,'rad'=8] {'rad'}, dimensions={0}, use_global_device_ids=true | all-gather | bytes 55296 | tf_op jit(solution)/shard_map/all_gather | solution.py:196
  396.8 7.2 %fusion.99 = f32[8,1,192,1]{2,1,3,0:T(1,128)S(1)} fusion(f32[8,4,192,1]{2,3,1,0:T(1,128)S(1)} %reshape.333, f32[8,4,192,192]{3,2,1,0:T(8,128)} %param.23), kind=kOutput, calls=%fused_computation.176 | convolution fusion | flops 14155776 | bytes 4749312 | tf_op jit(solution)/shard_map/bnij,bnj->bi/dot_general | solution.py:199
  (326 shorter events, 213.3 us)
Async XLA Ops:
  7.2 235.6 %copy-start = (f32[8,192,192]{2,1,0:T(8,128)S(1)}, f32[8,192,192]{2,1,0:T(8,128)}, u32[]{:S(2)}) copy-start(f32[8,192,192]{2,1,0:T(8,128)} %param.25) | copy-start | bytes 3538948
  7.2 234.2 %reduce-scatter.4.cloned.1.call-start = ((), (), s32[]{:S(2)}) async-start(), calls=%async_computation.1 | async-start | bytes 1769472
  11.5 26.7 %copy-start.4 = (s32[16384]{0:T(1024)S(1)}, s32[16384]{0:T(1024)}, u32[]{:S(2)}) copy-start(s32[16384]{0:T(1024)} %param.20) | copy-start | bytes 196612
  11.5 26.7 %copy-start.1 = (f32[3,16384]{1,0:T(4,128)S(1)}, f32[3,16384]{1,0:T(4,128)}, u32[]{:S(2)}) copy-start(f32[3,16384]{1,0:T(4,128)} %param.16) | copy-start | bytes 589828
  11.5 27.1 %copy-start.5 = (f32[3,16384]{1,0:T(4,128)S(1)}, f32[3,16384]{1,0:T(4,128)}, u32[]{:S(2)}) copy-start(f32[3,16384]{1,0:T(4,128)} %param.17) | copy-start | bytes 589828
  39.0 0.7 copy-start.2
  39.7 103.0 %copy-start.3 = (s32[16384]{0:T(1024)S(1)}, s32[16384]{0:T(1024)}, u32[]{:S(2)}) copy-start(s32[16384]{0:T(1024)} %param.19) | copy-start | bytes 196612
  132.2 6.2 %collective-permute-start.1 = (f32[8,1024]{1,0:T(8,128)S(1)}, f32[8,1024]{1,0:T(8,128)S(1)}, u32[]{:S(2)}, u32[]{:S(2)}) collective-permute-start(f32[8,1024]{1,0:T(8,128)S(1)} %bitcast.238), channel_id=1, source_target_pairs={{8,0},{16,8},{24,16},{9,1},{17,9},{25,17},{10,2},{18,10},{26,18},{... | collective-permute-start | bytes 98312 | tf_op jit(solution)/shard_map/ppermute | solution.py:19
  135.6 6.7 %collective-permute-start = (f32[8,1024]{1,0:T(8,128)S(1)}, f32[8,1024]{1,0:T(8,128)S(1)}, u32[]{:S(2)}, u32[]{:S(2)}) collective-permute-start(f32[8,1024]{1,0:T(8,128)S(1)} %bitcast.239), channel_id=1, source_target_pairs={{0,8},{8,16},{16,24},{1,9},{9,17},{17,25},{2,10},{10,18},{18,26},{... | collective-permute-start | bytes 98312 | tf_op jit(solution)/shard_map/ppermute | solution.py:19
  142.7 99.7 %copy-start.8 = (f32[384]{0:T(512)S(1)}, f32[384]{0:T(512)}, u32[]{:S(2)}) copy-start(f32[384]{0:T(512)} %param.21) | copy-start | bytes 4612
  142.7 99.9 %copy-start.6 = (f32[192,192]{1,0:T(8,128)S(1)}, f32[192,192]{1,0:T(8,128)}, u32[]{:S(2)}) copy-start(f32[192,192]{1,0:T(8,128)} %param.22) | copy-start | bytes 442372
  142.7 121.3 %copy-start.9 = (s32[8,4]{0,1:T(4,128)S(1)}, s32[8,4]{0,1:T(4,128)}, u32[]{:S(2)}) copy-start(s32[8,4]{0,1:T(4,128)} %param.24) | copy-start | bytes 388
  242.5 65.7 %copy-start.7 = (f32[4,384]{1,0:T(4,128)}, f32[4,384]{1,0:T(4,128)S(1)}, u32[]{:S(2)}) copy-start(f32[4,384]{1,0:T(4,128)S(1)} %broadcast_divide_fusion) | copy-start | bytes 18436
  258.2 6.2 %collective-permute-start.3 = (f32[64,192]{1,0:T(8,128)S(1)}, f32[64,192]{1,0:T(8,128)S(1)}, u32[]{:S(2)}, u32[]{:S(2)}) collective-permute-start(f32[64,192]{1,0:T(8,128)S(1)} %all_gather.15), channel_id=1, source_target_pairs={{8,0},{16,8},{24,16},{9,1},{17,9},{25,17},{10,2},{18,10},{26,18},{... | collective-permute-start | bytes 147464 | tf_op jit(solution)/shard_map/ppermute | solution.py:32
  261.8 7.1 %collective-permute-start.2 = (f32[64,192]{1,0:T(8,128)S(1)}, f32[64,192]{1,0:T(8,128)S(1)}, u32[]{:S(2)}, u32[]{:S(2)}) collective-permute-start(f32[64,192]{1,0:T(8,128)S(1)} %all_gather.15), channel_id=1, source_target_pairs={{0,8},{8,16},{16,24},{1,9},{9,17},{17,25},{2,10},{10,18},{18,26},{... | collective-permute-start | bytes 147464 | tf_op jit(solution)/shard_map/ppermute | solution.py:30
  291.7 6.2 %collective-permute-start.5 = (f32[64,192]{1,0:T(8,128)S(1)}, f32[64,192]{1,0:T(8,128)S(1)}, u32[]{:S(2)}, u32[]{:S(2)}) collective-permute-start(f32[64,192]{1,0:T(8,128)S(1)} %all_gather.16), channel_id=1, source_target_pairs={{8,0},{16,8},{24,16},{9,1},{17,9},{25,17},{10,2},{18,10},{26,18},{... | collective-permute-start | bytes 147464 | tf_op jit(solution)/shard_map/ppermute | solution.py:32
  293.6 7.1 %collective-permute-start.4 = (f32[64,192]{1,0:T(8,128)S(1)}, f32[64,192]{1,0:T(8,128)S(1)}, u32[]{:S(2)}, u32[]{:S(2)}) collective-permute-start(f32[64,192]{1,0:T(8,128)S(1)} %all_gather.16), channel_id=1, source_target_pairs={{0,8},{8,16},{16,24},{1,9},{9,17},{17,25},{2,10},{10,18},{18,26},{... | collective-permute-start | bytes 147464 | tf_op jit(solution)/shard_map/ppermute | solution.py:30
  323.8 6.2 %collective-permute-start.7 = (f32[64,192]{1,0:T(8,128)S(1)}, f32[64,192]{1,0:T(8,128)S(1)}, u32[]{:S(2)}, u32[]{:S(2)}) collective-permute-start(f32[64,192]{1,0:T(8,128)S(1)} %all_gather.17), channel_id=1, source_target_pairs={{8,0},{16,8},{24,16},{9,1},{17,9},{25,17},{10,2},{18,10},{26,18},{... | collective-permute-start | bytes 147464 | tf_op jit(solution)/shard_map/ppermute | solution.py:32
  325.7 7.1 %collective-permute-start.6 = (f32[64,192]{1,0:T(8,128)S(1)}, f32[64,192]{1,0:T(8,128)S(1)}, u32[]{:S(2)}, u32[]{:S(2)}) collective-permute-start(f32[64,192]{1,0:T(8,128)S(1)} %all_gather.17), channel_id=1, source_target_pairs={{0,8},{8,16},{16,24},{1,9},{9,17},{17,25},{2,10},{10,18},{18,26},{... | collective-permute-start | bytes 147464 | tf_op jit(solution)/shard_map/ppermute | solution.py:30
  355.7 6.2 %collective-permute-start.9 = (f32[64,192]{1,0:T(8,128)S(1)}, f32[64,192]{1,0:T(8,128)S(1)}, u32[]{:S(2)}, u32[]{:S(2)}) collective-permute-start(f32[64,192]{1,0:T(8,128)S(1)} %all_gather.18), channel_id=1, source_target_pairs={{8,0},{16,8},{24,16},{9,1},{17,9},{25,17},{10,2},{18,10},{26,18},{... | collective-permute-start | bytes 147464 | tf_op jit(solution)/shard_map/ppermute | solution.py:32
  357.6 7.1 %collective-permute-start.8 = (f32[64,192]{1,0:T(8,128)S(1)}, f32[64,192]{1,0:T(8,128)S(1)}, u32[]{:S(2)}, u32[]{:S(2)}) collective-permute-start(f32[64,192]{1,0:T(8,128)S(1)} %all_gather.18), channel_id=1, source_target_pairs={{0,8},{8,16},{16,24},{1,9},{9,17},{17,25},{2,10},{10,18},{18,26},{... | collective-permute-start | bytes 147464 | tf_op jit(solution)/shard_map/ppermute | solution.py:30
  387.5 6.5 %collective-permute-start.11 = (f32[64,192]{1,0:T(8,128)S(1)}, f32[64,192]{1,0:T(8,128)S(1)}, u32[]{:S(2)}, u32[]{:S(2)}) collective-permute-start(f32[64,192]{1,0:T(8,128)S(1)} %all_gather.19), channel_id=1, source_target_pairs={{8,0},{16,8},{24,16},{9,1},{17,9},{25,17},{10,2},{18,10},{26,18},{... | collective-permute-start | bytes 147464 | tf_op jit(solution)/shard_map/ppermute | solution.py:32
  389.5 7.1 %collective-permute-start.10 = (f32[64,192]{1,0:T(8,128)S(1)}, f32[64,192]{1,0:T(8,128)S(1)}, u32[]{:S(2)}, u32[]{:S(2)}) collective-permute-start(f32[64,192]{1,0:T(8,128)S(1)} %all_gather.19), channel_id=1, source_target_pairs={{0,8},{8,16},{16,24},{1,9},{9,17},{17,25},{2,10},{10,18},{18,26},{... | collective-permute-start | bytes 147464 | tf_op jit(solution)/shard_map/ppermute | solution.py:30
Sparse Core Ops, SparseCore 0:
  207.2 34.1 reduce-scatter.3
where the time goes:
time: 418 us; the launch traced here: 413 us
  matrix products  170 us (41%)
  blocking collectives  70.2 us (17%)
  other arithmetic  58 us (14%)
  waiting for transfers between devices  54.9 us (13%)
  starting transfers between devices  35 us (8%)
  between operations  14.9 us (4%)
  local copies, waits for them, and re-layouts  7.52 us (2%)
    dot_general x25, matrix products, spread_block(): lax.dot_general(spread, hot_upper, (((1,), (1,)), ((), ())), precision=hi...  100 us
    all_gather x5, blocking collectives, body(): gathered = lax.all_gather(velocity, 'rad', axis=0, tiled=True)  70.2 us
    mul x25, other arithmetic, spread_block(): spread = (values[:, None, :] * hot_lower[None]).reshape(rows * 128, size)  39.8 us
    dot_general x5, matrix products, body(): image = jnp.einsum('bnij,bnj->bi', stiffness, neighbours, precision=highest)  35.9 us
    unnamed x2, waiting for transfers between devices  34.3 us
    dot_general x8, matrix products, one_block(): jnp.dot(arranged, hot_upper, precision=highest).reshape(rows, 128, size)  18.2 us
    ppermute x5, starting transfers between devices, extended(): lax.ppermute(tail, axis, [(i, (i + 1) % count) for i in range(ends)])  17.9 us
    ppermute x5, waiting for transfers between devices, extended(): lax.ppermute(tail, axis, [(i, (i + 1) % count) for i in range(ends)])  15.5 us
  transfers between devices with their start and end apart: 13, of which 11 were waited for; matrix products, arithmetic and copies ran while one was open for 0% of the time, Pallas kernels for 0%

commit v1 on v0

--- a/solution.py
+++ b/solution.py
@@ -193,7 +193,14 @@
     ).astype(jnp.float32)
     velocity = damping * precondition(force)
     for sweep_index in range(1, ITERS):
-        gathered = lax.all_gather(velocity, "rad", axis=0, tiled=True)
+        ring = [velocity]
+        for hop in range(7):
+            ring.append(lax.ppermute(ring[-1], "rad", [(dev, (dev + 1) % 8) for dev in range(8)]))
+        gathered = jnp.roll(
+            jnp.concatenate(ring[::-1], axis=0),
+            (lax.axis_index("rad") + 1) * ring[0].shape[0],
+            axis=0,
+        )
         window = extended(gathered, (("slab", 0),), gathered.shape[0])
         neighbours = jnp.dot(selector, window, precision=highest).reshape(own_blocks, -1, BLOCK)
         image = jnp.einsum("bnij,bnj->bi", stiffness, neighbours, precision=highest)

time: 418 us -> 520 us (1.24)
  waiting for transfers between devices: 54.9 us -> 225 us
  blocking collectives: 70.2 us -> 0 us
    ppermute x0 -> x35, waiting for transfers between devices: none -> 171 us  [body(): lax.ppermute(ring[-1], 'rad', [(dev, (dev + 1) % 8) for dev in range(8)])]
    all_gather x5 -> x0, blocking collectives: 70.2 us -> none  [body(): gathered = lax.all_gather(velocity, 'rad', axis=0, tiled=True)]
  transfers between devices with their start and end apart: 13 -> 48, of which waited for: 11 -> 46; matrix products, arithmetic and copies ran while one was open for 0% -> 0% of each run, Pallas kernels for 0% -> 0%
where the time goes in v1:
time: 520 us; the launch traced here: 515 us
  waiting for transfers between devices  225 us (43%)
  matrix products  171 us (33%)
  other arithmetic  58.7 us (11%)
  starting transfers between devices  35.5 us (7%)
  between operations  15.2 us (3%)
  local copies, waits for them, and re-layouts  7.62 us (1%)
    ppermute x35, waiting for transfers between devices, body(): lax.ppermute(ring[-1], 'rad', [(dev, (dev + 1) % 8) for dev in range(8)])  171 us
    dot_general x25, matrix products, spread_block(): lax.dot_general(spread, hot_upper, (((1,), (1,)), ((), ())), precision=hi...  100 us
    mul x25, other arithmetic, spread_block(): spread = (values[:, None, :] * hot_lower[None]).reshape(rows * 128, size)  40.3 us
    dot_general x5, matrix products, body(): image = jnp.einsum('bnij,bnj->bi', stiffness, neighbours, precision=highest)  36.2 us
    unnamed x2, waiting for transfers between devices  34.6 us
    ppermute x5, starting transfers between devices, extended(): lax.ppermute(tail, axis, [(i, (i + 1) % count) for i in range(ends)])  18.4 us
    dot_general x8, matrix products, one_block(): jnp.dot(arranged, hot_upper, precision=highest).reshape(rows, 128, size)  18.2 us
    ppermute x5, waiting for transfers between devices, extended(): lax.ppermute(tail, axis, [(i, (i + 1) % count) for i in range(ends)])  15 us
  transfers between devices with their start and end apart: 48, of which 46 were waited for; matrix products, arithmetic and copies ran while one was open for 0% of the time, Pallas kernels for 0%

profile of v1, /device:TPU:4, one launch (start us, length us, event | category | flops | bytes accessed | tf_op | source)
XLA Modules:
  0.0 514.9 jit_solution(7177508204410388123)
XLA Ops:
  11.6 26.4 %while.41 = (s32[]{:T(128)}, f32[8,5,2048]{2,1,0:T(8,128)S(1)}, s32[8,2048]{1,0:T(8,128)S(1)}, f32[640,24]{0,1:T(8,128)S(1)}, s32[]{:T(128)}) while((s32[]{:T(128)}, f32[8,5,2048]{2,1,0:T(8,128)S(1)}, s32[8,2048]{1,0:T(8,128)S(1)}, f32[640,24]{0,1:T(8,128)S(1)}, s32[]{:T(128)}) %tuple.141), condition=%wide.region_2.3_spmd, body=%wide.region_0.2_spmd.sunk | while | flops 380719104 | bytes 12882001 | solution.py:91
  39.7 92.6 %while.42 = (s32[]{:T(128)}, s32[2]{0:T(128)S(1)}, f32[2,1024,8]{1,2,0:T(8,128)S(1)}, s32[8,2048]{1,0:T(8,128)S(1)}, f32[8,8,2048]{2,1,0:T(8,128)S(1)}, /*index=5*/s32[]{:T(128)}, s32[]{:T(128)}) while((s32[]{:T(128)}, s32[2]{0:T(128)S(1)}, f32[2,1024,8]{1,2,0:T(8,128)S(1)}, s32[8,2048]{1,0:T(8,128)S(1)}, ...), condition=%wide.region_5.6_spmd.clone, body=%wide.region_3.5_spmd.clone.sunk | while | flops 433287168 | bytes 38502552 | solution.py:144
  142.8 63.1 %while.43 = (s32[]{:T(128)}, f32[512,24]{0,1:T(8,128)S(1)}, f32[9,4,2048]{2,0,1:T(8,128)S(1)}, s32[9,2048]{1,0:T(8,128)S(1)}, s32[]{:T(128)}, /*index=5*/s32[]{:T(128)}) while((s32[]{:T(128)}, f32[512,24]{0,1:T(8,128)S(1)}, f32[9,4,2048]{2,0,1:T(8,128)S(1)}, s32[9,2048]{1,0:T(8,128)S(1)}, s32[]{:T(128)}, ...), condition=%wide.region_7.8_spmd.clone, body=%wide.region_6.7_spmd.clone.sunk | while | flops 303677440 | bytes 10805343 | solution.py:116
  207.6 34.6 %reduce-scatter.4.cloned.1.call-done = f32[384,4]{1,0:T(8,128)} async-done(((f32[3072,4]{1,0:T(8,128)}), f32[384,4]{1,0:T(8,128)}) %reduce-scatter.4.cloned.1.call-update) | async-done | bytes 6160
  245.1 4.9 collective-permute-done.2
  250.0 4.9 collective-permute-done.3
  264.6 4.9 collective-permute-done.6
  269.5 4.9 collective-permute-done.7
  274.3 4.9 collective-permute-done.8
  289.8 7.2 %fusion.100 = f32[8,1,192,1]{2,1,3,0:T(1,128)S(1)} fusion(f32[8,4,192,1]{2,3,1,0:T(1,128)S(1)} %reshape.325, f32[8,4,192,192]{3,2,1,0:T(8,128)} %param.25), kind=kOutput, calls=%fused_computation.227 | convolution fusion | flops 14155776 | bytes 4749312 | tf_op jit(solution)/shard_map/bnij,bnj->bi/dot_general | solution.py:206
  298.4 4.9 collective-permute-done.11
  313.0 4.9 collective-permute-done.14
  317.9 4.9 collective-permute-done.15
  322.8 4.9 collective-permute-done.16
  327.6 4.9 collective-permute-done.17
  341.9 7.4 %fusion.101 = f32[8,1,192,1]{2,1,3,0:T(1,128)S(1)} fusion(f32[8,4,192,1]{2,3,1,0:T(1,128)S(1)} %reshape.327, f32[8,4,192,192]{3,2,1,0:T(8,128)} %param.25), kind=kOutput, calls=%fused_computation.228 | convolution fusion | flops 14155776 | bytes 4749312 | tf_op jit(solution)/shard_map/bnij,bnj->bi/dot_general | solution.py:206
  350.7 4.9 collective-permute-done.20
  355.6 4.9 collective-permute-done.21
  375.1 4.9 collective-permute-done.25
  394.2 7.2 %fusion.102 = f32[8,1,192,1]{2,1,3,0:T(1,128)S(1)} fusion(f32[8,4,192,1]{2,3,1,0:T(1,128)S(1)} %reshape.329, f32[8,4,192,192]{3,2,1,0:T(8,128)} %param.25), kind=kOutput, calls=%fused_computation.229 | convolution fusion | flops 14155776 | bytes 4749312 | tf_op jit(solution)/shard_map/bnij,bnj->bi/dot_general | solution.py:206
  402.8 4.9 collective-permute-done.29
  446.3 7.2 %fusion.103 = f32[8,1,192,1]{2,1,3,0:T(1,128)S(1)} fusion(f32[8,4,192,1]{2,3,1,0:T(1,128)S(1)} %reshape.331, f32[8,4,192,192]{3,2,1,0:T(8,128)} %param.25), kind=kOutput, calls=%fused_computation.230 | convolution fusion | flops 14155776 | bytes 4749312 | tf_op jit(solution)/shard_map/bnij,bnj->bi/dot_general | solution.py:206
  454.9 4.9 collective-permute-done.38
  498.6 7.2 %fusion.104 = f32[8,1,192,1]{2,1,3,0:T(1,128)S(1)} fusion(f32[8,4,192,1]{2,3,1,0:T(1,128)S(1)} %reshape.333, f32[8,4,192,192]{3,2,1,0:T(8,128)} %param.25), kind=kOutput, calls=%fused_computation.231 | convolution fusion | flops 14155776 | bytes 4749312 | tf_op jit(solution)/shard_map/bnij,bnj->bi/dot_general | solution.py:206
  (436 shorter events, 353.4 us)
Async XLA Ops:
  7.2 235.1 %reduce-scatter.4.cloned.1.call-start = ((), (), s32[]{:S(2)}) async-start(), calls=%async_computation.1 | async-start | bytes 1769472
  132.3 6.2 %collective-permute-start.1 = (f32[8,1024]{1,0:T(8,128)S(1)}, f32[8,1024]{1,0:T(8,128)S(1)}, u32[]{:S(2)}, u32[]{:S(2)}) collective-permute-start(f32[8,1024]{1,0:T(8,128)S(1)} %bitcast.240), channel_id=1, source_target_pairs={{8,0},{16,8},{24,16},{9,1},{17,9},{25,17},{10,2},{18,10},{26,18},{... | collective-permute-start | bytes 98312 | tf_op jit(solution)/shard_map/ppermute | solution.py:19
  135.7 6.7 %collective-permute-start = (f32[8,1024]{1,0:T(8,128)S(1)}, f32[8,1024]{1,0:T(8,128)S(1)}, u32[]{:S(2)}, u32[]{:S(2)}) collective-permute-start(f32[8,1024]{1,0:T(8,128)S(1)} %bitcast.241), channel_id=1, source_target_pairs={{0,8},{8,16},{16,24},{1,9},{9,17},{17,25},{2,10},{10,18},{18,26},{... | collective-permute-start | bytes 98312 | tf_op jit(solution)/shard_map/ppermute | solution.py:19
  245.1 4.9 collective-permute-start.2
  250.0 4.9 collective-permute-start.3
  269.5 4.9 collective-permute-start.7
  274.3 4.9 collective-permute-start.8
  279.3 6.2 %collective-permute-start.10 = (f32[64,192]{1,0:T(8,128)S(1)}, f32[64,192]{1,0:T(8,128)S(1)}, u32[]{:S(2)}, u32[]{:S(2)}) collective-permute-start(f32[64,192]{1,0:T(8,128)S(1)} %fusion.62), channel_id=1, source_target_pairs={{8,0},{16,8},{24,16},{9,1},{17,9},{25,17},{10,2},{18,10},{26,18},{... | collective-permute-start | bytes 147464 | tf_op jit(solution)/shard_map/ppermute | solution.py:32
  282.4 7.1 %collective-permute-start.9 = (f32[64,192]{1,0:T(8,128)S(1)}, f32[64,192]{1,0:T(8,128)S(1)}, u32[]{:S(2)}, u32[]{:S(2)}) collective-permute-start(f32[64,192]{1,0:T(8,128)S(1)} %fusion.62), channel_id=1, source_target_pairs={{0,8},{8,16},{16,24},{1,9},{9,17},{17,25},{2,10},{10,18},{18,26},{... | collective-permute-start | bytes 147464 | tf_op jit(solution)/shard_map/ppermute | solution.py:30
  298.4 4.9 collective-permute-start.11
  317.9 4.9 collective-permute-start.15
  322.8 4.9 collective-permute-start.16
  332.6 6.2 %collective-permute-start.19 = (f32[64,192]{1,0:T(8,128)S(1)}, f32[64,192]{1,0:T(8,128)S(1)}, u32[]{:S(2)}, u32[]{:S(2)}) collective-permute-start(f32[64,192]{1,0:T(8,128)S(1)} %fusion.61), channel_id=1, source_target_pairs={{8,0},{16,8},{24,16},{9,1},{17,9},{25,17},{10,2},{18,10},{26,18},{... | collective-permute-start | bytes 147464 | tf_op jit(solution)/shard_map/ppermute | solution.py:32
  334.6 7.1 %collective-permute-start.18 = (f32[64,192]{1,0:T(8,128)S(1)}, f32[64,192]{1,0:T(8,128)S(1)}, u32[]{:S(2)}, u32[]{:S(2)}) collective-permute-start(f32[64,192]{1,0:T(8,128)S(1)} %fusion.61), channel_id=1, source_target_pairs={{0,8},{8,16},{16,24},{1,9},{9,17},{17,25},{2,10},{10,18},{18,26},{... | collective-permute-start | bytes 147464 | tf_op jit(solution)/shard_map/ppermute | solution.py:30
  350.7 4.9 collective-permute-start.20
  384.9 6.2 %collective-permute-start.28 = (f32[64,192]{1,0:T(8,128)S(1)}, f32[64,192]{1,0:T(8,128)S(1)}, u32[]{:S(2)}, u32[]{:S(2)}) collective-permute-start(f32[64,192]{1,0:T(8,128)S(1)} %fusion.60), channel_id=1, source_target_pairs={{8,0},{16,8},{24,16},{9,1},{17,9},{25,17},{10,2},{18,10},{26,18},{... | collective-permute-start | bytes 147464 | tf_op jit(solution)/shard_map/ppermute | solution.py:32
  386.9 7.1 %collective-permute-start.27 = (f32[64,192]{1,0:T(8,128)S(1)}, f32[64,192]{1,0:T(8,128)S(1)}, u32[]{:S(2)}, u32[]{:S(2)}) collective-permute-start(f32[64,192]{1,0:T(8,128)S(1)} %fusion.60), channel_id=1, source_target_pairs={{0,8},{8,16},{16,24},{1,9},{9,17},{17,25},{2,10},{10,18},{18,26},{... | collective-permute-start | bytes 147464 | tf_op jit(solution)/shard_map/ppermute | solution.py:30
  402.8 4.9 collective-permute-start.29
  437.0 6.2 %collective-permute-start.37 = (f32[64,192]{1,0:T(8,128)S(1)}, f32[64,192]{1,0:T(8,128)S(1)}, u32[]{:S(2)}, u32[]{:S(2)}) collective-permute-start(f32[64,192]{1,0:T(8,128)S(1)} %fusion.59), channel_id=1, source_target_pairs={{8,0},{16,8},{24,16},{9,1},{17,9},{25,17},{10,2},{18,10},{26,18},{... | collective-permute-start | bytes 147464 | tf_op jit(solution)/shard_map/ppermute | solution.py:32
  439.0 7.1 %collective-permute-start.36 = (f32[64,192]{1,0:T(8,128)S(1)}, f32[64,192]{1,0:T(8,128)S(1)}, u32[]{:S(2)}, u32[]{:S(2)}) collective-permute-start(f32[64,192]{1,0:T(8,128)S(1)} %fusion.59), channel_id=1, source_target_pairs={{0,8},{8,16},{16,24},{1,9},{9,17},{17,25},{2,10},{10,18},{18,26},{... | collective-permute-start | bytes 147464 | tf_op jit(solution)/shard_map/ppermute | solution.py:30
  454.9 4.9 collective-permute-start.38
  484.1 5.1 collective-permute-start.44
  489.3 6.5 %collective-permute-start.46 = (f32[64,192]{1,0:T(8,128)S(1)}, f32[64,192]{1,0:T(8,128)S(1)}, u32[]{:S(2)}, u32[]{:S(2)}) collective-permute-start(f32[64,192]{1,0:T(8,128)S(1)} %fusion.58), channel_id=1, source_target_pairs={{8,0},{16,8},{24,16},{9,1},{17,9},{25,17},{10,2},{18,10},{26,18},{... | collective-permute-start | bytes 147464 | tf_op jit(solution)/shard_map/ppermute | solution.py:32
  491.3 7.1 %collective-permute-start.45 = (f32[64,192]{1,0:T(8,128)S(1)}, f32[64,192]{1,0:T(8,128)S(1)}, u32[]{:S(2)}, u32[]{:S(2)}) collective-permute-start(f32[64,192]{1,0:T(8,128)S(1)} %fusion.58), channel_id=1, source_target_pairs={{0,8},{8,16},{16,24},{1,9},{9,17},{17,25},{2,10},{10,18},{18,26},{... | collective-permute-start | bytes 147464 | tf_op jit(solution)/shard_map/ppermute | solution.py:30
  (34 other events, 987.4 us)
Sparse Core Ops, SparseCore 0:
  207.8 34.4 reduce-scatter.3
